TPU v7x, 512 devices: a whole 4x4x16 slice. The times are simulated.
512 devices in a mesh: ctx: 32 (over z, core), head: 16 (over x, y).
Axes of the slice: x: 4, y: 4, z: 16, core: 2. Of those that a mesh axis runs over, the one named last changes fastest.
Arguments:
- attn_q: bfloat16 [4096, 4096], P('ctx', 'head'), may hold values from -6 to 6
- attn_k: bfloat16 [4096, 512], P('ctx'), may hold values from -6 to 6
- attn_v: bfloat16 [4096, 512], P('ctx'), may hold values from -0.375 to 0.375
- attn_cot: bfloat16 [4096, 4096], P('ctx', 'head'), may hold values from -6 to 6
- attn_lse: float32 [16, 4096], P('head'), may hold values from 3 to 6
- attn_delta: float32 [16, 4096], P('head'), may hold values from -6 to 6
- block_lists: int32 [16, 64, 4], P('head'), may hold values from 0 to 63, as said below
- gdn_q: bfloat16 [4096, 2048], P('ctx', 'head'), may hold values from -6 to 6
- gdn_k: bfloat16 [4096, 2048], P('ctx', 'head'), may hold values from -6 to 6
- gdn_v: bfloat16 [4096, 4096], P('ctx', 'head'), may hold values from -6 to 6
- decay_logit: float32 [32, 4096], P('head', 'ctx'), may hold values from -8 to 8
- write_logit: float32 [32, 4096], P('head', 'ctx'), may hold values from -6 to 6
- decay_rate: float32 [32], P('head'), may hold values from 0.00024414062 to 0.1
- write_scale: float32 [32], P('head'), may hold values from 0.05 to 1
- gdn_cot: bfloat16 [4096, 4096], P('ctx', 'head'), may hold values from -6 to 6
Outputs:
- attn_dq: float32 [4096, 4096], P('ctx', 'head')
- attn_dk: float32 [4096, 512], P('ctx')
- attn_dv: float32 [4096, 512], P('ctx')
- gdn_dq: float32 [4096, 2048], P('ctx', 'head')
- gdn_dk: float32 [4096, 2048], P('ctx', 'head')
- gdn_dv: float32 [4096, 4096], P('ctx', 'head')
- gdn_ddecay: float32 [32, 4096], P('head', 'ctx')
- gdn_dwrite: float32 [32, 4096], P('head', 'ctx')
Inputs may be any that keep to these rules, and one draw needn't show every extreme that they name: `block_lists`: entries for query block b lie in 0 to b and may repeat.
All inputs are finite; a program needn't handle non-finite values.
Results may differ from a plain program's by a relative error of at most 0.00035.
Values may be sent and summed in bfloat16 or wider, within the bound.
No kernel may reach another device: no remote copies, remote signals or barrier semaphores. Data moves between devices by JAX's collectives and lax.ppermute only.
A program may use at most 128 MiB of HBM per device.

v0:
```python
import jax
import jax.numpy as jnp
from jax import lax
from jax.sharding import PartitionSpec as P

Q_HEADS = 16
KV_HEADS = 2
HD = 256
GDIM = 128
BLK = 64
TOPK = 4
SPAN = 64
HIGHEST = lax.Precision.HIGHEST


def prefix(value, axis, join, neutral, backward):
    count, mine = (lax.axis_size(axis), lax.axis_index(axis))
    pieces = jax.tree.map(lambda part: lax.all_gather(part, axis), value)
    if backward:
        pieces = jax.tree.map(lambda part: part[::-1], pieces)
        mine = count - 1 - mine
    so_far = jax.tree.map(
        lambda part, zero: jnp.full_like(part, 0) + jnp.asarray(zero, part.dtype), value, neutral
    )

    def turn(position, so_far):
        longer = join(so_far, jax.tree.map(lambda part: part[position], pieces))
        return jax.tree.map(lambda new, old: jnp.where(position < mine, new, old), longer, so_far)

    return lax.fori_loop(0, count - 1, turn, so_far)


def unit_rows(matrix):
    return matrix / jnp.sqrt(jnp.sum(matrix * matrix, axis=-1, keepdims=True) + 1e-06)


def span_update(memory, packed):
    queries, keys_in, values_in, log_decay, write_gain = packed
    length = log_decay.shape[-1]
    cum_log = jnp.cumsum(log_decay, axis=-1)
    log_gap = cum_log[:, :, None] - cum_log[:, None, :]
    order_ids = jnp.arange(length)
    strict_low = order_ids[:, None] > order_ids[None, :]
    with_diag = order_ids[:, None] >= order_ids[None, :]
    decay_strict = jnp.where(strict_low, jnp.exp(jnp.where(strict_low, log_gap, 0.0)), 0.0)
    decay_upto = jnp.where(with_diag, jnp.exp(jnp.where(with_diag, log_gap, 0.0)), 0.0)
    key_gram = jnp.einsum("htd,hsd->hts", keys_in, keys_in, precision=HIGHEST)
    system = write_gain[:, :, None] * decay_strict * key_gram + jnp.eye(length, dtype=jnp.float32)
    decay_now = jnp.exp(cum_log)
    recalled = jnp.einsum("hvd,htd->htv", memory, keys_in, precision=HIGHEST)
    target = write_gain[:, :, None] * (values_in - decay_now[:, :, None] * recalled)
    written = lax.linalg.triangular_solve(
        system, target, left_side=True, lower=True, unit_diagonal=True
    )
    read_old = jnp.einsum("hvd,htd->htv", memory, queries, precision=HIGHEST)
    query_key = jnp.einsum("htd,hsd->hts", queries, keys_in, precision=HIGHEST)
    outputs = decay_now[:, :, None] * read_old + jnp.einsum(
        "hts,hsv->htv", decay_upto * query_key, written, precision=HIGHEST
    )
    tail_decay = jnp.exp(cum_log[:, -1:] - cum_log)
    memory_next = jnp.exp(cum_log[:, -1])[:, None, None] * memory + jnp.einsum(
        "hsv,hsd->hvd", written * tail_decay[:, :, None], keys_in, precision=HIGHEST
    )
    return (memory_next, outputs)


def delta_forward(raw_inputs, memory, rate_heads, scale_heads):
    query_raw, key_raw, value_raw, decay_in, write_in = raw_inputs
    n_tokens = query_raw.shape[0]
    key_heads = query_raw.shape[1] // GDIM
    value_heads = value_raw.shape[1] // GDIM
    ratio_heads = value_heads // key_heads
    n_spans = n_tokens // SPAN
    queries = jnp.repeat(
        unit_rows(query_raw.reshape(n_tokens, key_heads, GDIM)), ratio_heads, axis=1
    )
    keys_norm = jnp.repeat(
        unit_rows(key_raw.reshape(n_tokens, key_heads, GDIM)), ratio_heads, axis=1
    )
    values_in = value_raw.reshape(n_tokens, value_heads, GDIM)
    log_decay = -rate_heads[:, None] * jax.nn.softplus(decay_in)
    write_gain = scale_heads[:, None] * jax.nn.sigmoid(write_in)

    def blocks_of(tensor):
        return tensor.reshape(n_spans, SPAN, value_heads, GDIM).transpose(0, 2, 1, 3)

    def gates_of(tensor):
        return tensor.reshape(value_heads, n_spans, SPAN).transpose(1, 0, 2)

    memory_end, outputs = lax.scan(
        span_update,
        memory,
        (
            blocks_of(queries),
            blocks_of(keys_norm),
            blocks_of(values_in),
            gates_of(log_decay),
            gates_of(write_gain),
        ),
    )
    return (outputs.transpose(0, 2, 1, 3).reshape(n_tokens, value_heads * GDIM), memory_end)


def sparse_query_grad(
    q_blocks,
    cot_blocks,
    own_keys,
    own_values,
    listed_keys,
    listed_values,
    lse_rows,
    delta_rows,
    head_lists,
    block_ids,
):
    score_scale = HD ** (-0.5)
    position = jnp.arange(BLK)
    causal = position[:, None] >= position[None, :]
    slot_ids = jnp.arange(TOPK)
    repeated = jnp.any(
        (head_lists[:, :, None] == head_lists[:, None, :])
        & (slot_ids[:, None] > slot_ids[None, :]),
        axis=2,
    )
    usable = (head_lists < block_ids[:, None]) & jnp.logical_not(repeated)
    own_score = (
        jnp.einsum("bid,bjd->bij", q_blocks, own_keys, preferred_element_type=jnp.float32)
        * score_scale
    )
    list_score = (
        jnp.einsum("bid,btjd->bitj", q_blocks, listed_keys, preferred_element_type=jnp.float32)
        * score_scale
    )
    own_prob = jnp.where(causal[None], jnp.exp(own_score - lse_rows[:, :, None]), 0.0)
    list_prob = jnp.where(
        usable[:, None, :, None], jnp.exp(list_score - lse_rows[:, :, None, None]), 0.0
    )
    own_dprob = jnp.einsum(
        "bid,bjd->bij", cot_blocks, own_values, preferred_element_type=jnp.float32
    )
    list_dprob = jnp.einsum(
        "bid,btjd->bitj", cot_blocks, listed_values, preferred_element_type=jnp.float32
    )
    own_dscore = own_prob * (own_dprob - delta_rows[:, :, None])
    list_dscore = list_prob * (list_dprob - delta_rows[:, :, None, None])
    own_part = jnp.einsum(
        "bij,bjd->bid", own_dscore, own_keys.astype(jnp.float32), precision=HIGHEST
    )
    list_part = jnp.einsum(
        "bitj,btjd->bid", list_dscore, listed_keys.astype(jnp.float32), precision=HIGHEST
    )
    return (own_part + list_part) * score_scale


def compose_maps(earlier, later):
    product = jnp.einsum("hij,hjk->hik", earlier[0], later[0], precision=HIGHEST)
    shifted = jnp.einsum("hij,hjk->hik", earlier[1], later[0], precision=HIGHEST) + later[1]
    return (product, shifted)


def on_device(
    attn_q,
    attn_k,
    attn_v,
    attn_cot,
    attn_lse,
    attn_delta,
    block_lists,
    gdn_q,
    gdn_k,
    gdn_v,
    decay_logit,
    write_logit,
    decay_rate,
    write_scale,
    gdn_cot,
):
    score_scale = HD ** (-0.5)
    head_index = lax.axis_index("head")
    ctx_index = lax.axis_index("ctx")
    tok_rows = attn_q.shape[0]
    local_heads = attn_q.shape[1] // HD
    blocks_here = tok_rows // BLK
    kv_group = head_index * local_heads // (Q_HEADS // KV_HEADS)
    own_keys = lax.dynamic_index_in_dim(
        attn_k.reshape(tok_rows, KV_HEADS, HD), kv_group, 1, keepdims=False
    )
    own_values = lax.dynamic_index_in_dim(
        attn_v.reshape(tok_rows, KV_HEADS, HD), kv_group, 1, keepdims=False
    )
    row_base = ctx_index * tok_rows
    first_block = ctx_index * blocks_here
    key_block_ids = first_block + jnp.arange(blocks_here, dtype=jnp.int32)
    member = jnp.any(block_lists[:, :, :, None] == key_block_ids[None, None, None, :], axis=2)
    member_rows = jnp.repeat(jnp.repeat(member, BLK, axis=1), BLK, axis=2)
    key_pos = row_base + jnp.arange(tok_rows, dtype=jnp.int32)
    key_block = key_pos // BLK
    keys_whole, values_whole = (
        lax.all_gather(own_keys, "ctx", axis=0, tiled=True),
        lax.all_gather(own_values, "ctx", axis=0, tiled=True),
    )
    lists_own = lax.dynamic_slice_in_dim(block_lists, first_block, blocks_here, 1)
    lse_own = lax.dynamic_slice_in_dim(attn_lse, row_base, tok_rows, 1).reshape(
        local_heads, blocks_here, BLK
    )
    delta_own = lax.dynamic_slice_in_dim(attn_delta, row_base, tok_rows, 1).reshape(
        local_heads, blocks_here, BLK
    )
    q_blocks = attn_q.reshape(blocks_here, BLK, local_heads, HD).transpose(2, 0, 1, 3)
    cot_blocks = attn_cot.reshape(blocks_here, BLK, local_heads, HD).transpose(2, 0, 1, 3)
    listed_keys = keys_whole.reshape(-1, BLK, HD)[lists_own]
    listed_values = values_whole.reshape(-1, BLK, HD)[lists_own]
    grad_blocks = jax.vmap(sparse_query_grad, in_axes=(0, 0, None, None, 0, 0, 0, 0, 0, None))(
        q_blocks,
        cot_blocks,
        own_keys.reshape(blocks_here, BLK, HD),
        own_values.reshape(blocks_here, BLK, HD),
        listed_keys,
        listed_values,
        lse_own,
        delta_own,
        lists_own,
        key_block_ids,
    )
    grad_q = grad_blocks.transpose(1, 2, 0, 3).reshape(tok_rows, local_heads * HD)
    query_rows = lax.all_gather(attn_q, "ctx", axis=0, tiled=True)
    n_rows = query_rows.shape[0]
    queries = query_rows.reshape(n_rows, local_heads, HD)
    cotangent = lax.all_gather(attn_cot, "ctx", axis=0, tiled=True).reshape(n_rows, local_heads, HD)
    row_pos = jnp.arange(n_rows, dtype=jnp.int32)
    row_block = row_pos // BLK
    own_pair = (row_block[:, None] == key_block[None, :]) & (row_pos[:, None] >= key_pos[None, :])
    listed_pair = member_rows & (key_block[None, :] < row_block[:, None])[None]
    allowed = own_pair[None] | listed_pair
    scores = (
        jnp.einsum("nhd,kd->hnk", queries, own_keys, preferred_element_type=jnp.float32)
        * score_scale
    )
    prob_full = jnp.where(allowed, jnp.exp(scores - attn_lse[:, :, None]), 0.0)
    dprobs = jnp.einsum("nhd,kd->hnk", cotangent, own_values, preferred_element_type=jnp.float32)
    dscores = prob_full * (dprobs - attn_delta[:, :, None])
    grad_value = jnp.einsum(
        "hnk,nhd->kd", prob_full, cotangent.astype(jnp.float32), precision=HIGHEST
    )
    grad_key = (
        jnp.einsum("hnk,nhd->kd", dscores, queries.astype(jnp.float32), precision=HIGHEST)
        * score_scale
    )
    slot_mask = (jnp.arange(KV_HEADS) == kv_group)[None, :, None]
    key_slots = jnp.where(slot_mask, grad_key[:, None, :], 0.0).reshape(tok_rows, KV_HEADS * HD)
    value_slots = jnp.where(slot_mask, grad_value[:, None, :], 0.0).reshape(tok_rows, KV_HEADS * HD)
    attn_dk, attn_dv = lax.psum((key_slots, value_slots), "head")
    raw_inputs = (
        gdn_q.astype(jnp.float32),
        gdn_k.astype(jnp.float32),
        gdn_v.astype(jnp.float32),
        decay_logit,
        write_logit,
    )
    value_heads = gdn_v.shape[1] // GDIM
    zero_memory = jnp.zeros((value_heads, GDIM, GDIM), jnp.float32)
    unit_memory = jnp.broadcast_to(jnp.eye(GDIM, dtype=jnp.float32), zero_memory.shape)

    def local_run(raw_values, memory):
        return delta_forward(raw_values, memory, decay_rate, write_scale)

    silent_inputs = (
        raw_inputs[0],
        raw_inputs[1],
        jnp.zeros_like(raw_inputs[2]),
        raw_inputs[3],
        raw_inputs[4],
    )
    transition = local_run(silent_inputs, unit_memory)[1]
    outputs_zero, pull_zero = jax.vjp(local_run, raw_inputs, zero_memory)
    written_end = outputs_zero[1]
    cot_full = gdn_cot.astype(jnp.float32)
    local_grad = pull_zero((cot_full, zero_memory))[1]
    memory_in = prefix(
        (transition, written_end), "ctx", compose_maps, (unit_memory, zero_memory), False
    )[1]
    flipped = jnp.swapaxes(transition, 1, 2)
    memory_grad = prefix(
        (flipped, local_grad), "ctx", compose_maps, (unit_memory, zero_memory), True
    )[1]
    unused_out, pull_final = jax.vjp(local_run, raw_inputs, memory_in)
    grads = pull_final((cot_full, memory_grad))[0]
    return (grad_q, attn_dk, attn_dv, grads[0], grads[1], grads[2], grads[3], grads[4])


def solution(mesh):
    return jax.shard_map(
        on_device,
        mesh=mesh,
        in_specs=(
            P("ctx", "head"),
            P("ctx", None),
            P("ctx", None),
            P("ctx", "head"),
            P("head", None),
            P("head", None),
            P("head", None, None),
            P("ctx", "head"),
            P("ctx", "head"),
            P("ctx", "head"),
            P("head", "ctx"),
            P("head", "ctx"),
            P("head"),
            P("head"),
            P("ctx", "head"),
        ),
        out_specs=(
            P("ctx", "head"),
            P("ctx", None),
            P("ctx", None),
            P("ctx", "head"),
            P("ctx", "head"),
            P("ctx", "head"),
            P("head", "ctx"),
            P("head", "ctx"),
        ),
        check_vma=False,
    )
```

profile of v0, /device:TPU:1, one launch (start us, length us, event | category | flops | bytes accessed | tf_op | source)
XLA Modules:
  0.0 767.3 jit_solution(10239268752019939677)
XLA Ops:
  20.4 24.4 %while.177 = (s32[]{:T(128)}, f32[2,128,128]{2,1,0:T(8,128)S(1)}, f32[2,2,64,1]{2,1,3,0:T(2,128)S(1)}, f32[2,2,64,1]{2,1,3,0:T(2,128)S(1)}, f32[2,2,64,64]{3,2,1...) while((s32[]{:T(128)}, f32[2,128,128]{2,1,0:T(8,128)S(1)}, ...), condition=%wide.region_11.13_spmd.clone.clone, body=%wide.region_9.12_spmd.clone.clone.sunk | while | flops 88404160 | bytes 1473784 | solution.py:90
  21.7 9.9 %custom-call.48 = f32[2,1,64,64]{2,3,1,0:T(8,128)S(1)} custom-call(f32[2,1,64,64]{3,2,1,0:T(8,128)S(1)} %add_bitcast_fusion.8), custom_call_target="InvertDiagBlocksLowerTriangular" | custom-call | tf_op jit(solution)/shard_map/jvp()/while/body/eval_jaxpr/triangular_solve/custom-call.1 | solution.py:52
  33.9 9.9 %custom-call.48 = f32[2,1,64,64]{2,3,1,0:T(8,128)S(1)} custom-call(f32[2,1,64,64]{3,2,1,0:T(8,128)S(1)} %add_bitcast_fusion.8), custom_call_target="InvertDiagBlocksLowerTriangular" | custom-call | tf_op jit(solution)/shard_map/jvp()/while/body/eval_jaxpr/triangular_solve/custom-call.1 | solution.py:52
  45.5 23.5 %while.174 = (s32[]{:T(128)}, f32[2,128,128]{2,1,0:T(8,128)S(1)}, f32[2,2,1,1]{1,3,2,0:T(1,128)S(1)}, f32[2,2,64,1]{2,1,3,0:T(2,128)S(1)}, f32[2,2,64,128]{3,2,1...) while((s32[]{:T(128)}, f32[2,128,128]{2,1,0:T(8,128)S(1)}, ...), condition=%wide.region_13.16_spmd.clone, body=%wide.region_12.15_spmd.clone.sunk | while | flops 100954176 | bytes 1590971 | solution.py:90
  46.3 9.8 %custom-call.47 = f32[2,1,64,64]{2,3,1,0:T(8,128)S(1)} custom-call(f32[2,1,64,64]{3,2,1,0:T(8,128)S(1)} %fusion.505), custom_call_target="InvertDiagBlocksLowerTriangular" | custom-call | tf_op jit(solution)/shard_map/transpose(jvp())/while/body/eval_jaxpr/triangular_solve/custom-call.0 | solution.py:52
  58.1 9.8 %custom-call.47 = f32[2,1,64,64]{2,3,1,0:T(8,128)S(1)} custom-call(f32[2,1,64,64]{3,2,1,0:T(8,128)S(1)} %fusion.505), custom_call_target="InvertDiagBlocksLowerTriangular" | custom-call | tf_op jit(solution)/shard_map/transpose(jvp())/while/body/eval_jaxpr/triangular_solve/custom-call.0 | solution.py:52
  69.9 23.7 %while.171 = (s32[]{:T(128)}, f32[2,128,128]{2,1,0:T(8,128)S(1)}, f32[2,2,64]{2,1,0:T(2,128)S(1)}, f32[2,2,64]{2,1,0:T(2,128)S(1)}, f32[2,2,64,128]{3,2,1,0:T(8,128)S(1)}, /*index=5*/s32[]{:T(128)}, f32[]{:T(128)}) while((s32[]{:T(128)}, f32[2,128,128]{2,1,0:T(8,128)S(1)}, f32[2,2,64]{2,1,0:T(2,128)S(1)}, f32[2,2,64]{2,1,0:T(2,128)S(1)}, ...), condition=%wide.region_7.9_spmd, body=%wide.region_5.8_spmd.sunk | while | flops 75726912 | bytes 1051785 | solution.py:90
  71.1 9.8 %custom-call.43 = f32[2,1,64,64]{2,3,1,0:T(8,128)S(1)} custom-call(f32[2,1,64,64]{3,2,1,0:T(8,128)S(1)} %fusion.440), custom_call_target="InvertDiagBlocksLowerTriangular" | custom-call | tf_op jit(solution)/shard_map/while/body/eval_jaxpr/triangular_solve/custom-call.1 | solution.py:52
  83.0 9.8 %custom-call.43 = f32[2,1,64,64]{2,3,1,0:T(8,128)S(1)} custom-call(f32[2,1,64,64]{3,2,1,0:T(8,128)S(1)} %fusion.440), custom_call_target="InvertDiagBlocksLowerTriangular" | custom-call | tf_op jit(solution)/shard_map/while/body/eval_jaxpr/triangular_solve/custom-call.1 | solution.py:52
  102.2 2.9 fusion.267
  105.0 53.9 %all-gather.17.cloned.1.call-done = bf16[4096,256]{1,0:T(8,128)(2,1)} async-done(((bf16[128,256]{1,0:T(8,128)(2,1)}), bf16[4096,256]{1,0:T(8,128)(2,1)}) %all-gather.17.cloned.1.call-update) | async-done | bytes 2097168 | tf_op jit(solution)/shard_map/all_gather | solution.py:229
  158.9 2.6 fusion.271
  161.5 1.3 convolution_multiply_fusion.11
  165.2 66.4 %all-gather.21.cloned.1.call-done = bf16[4096,1,256]{0,2,1:T(8,128)(2,1)} async-done(((bf16[128,1,256]{0,2,1:T(8,128)(2,1)}), bf16[4096,1,256]{0,2,1:T(8,128)(2,1)}) %all-gather.21.cloned.1.call-update) | async-done | bytes 2097168 | tf_op jit(solution)/shard_map/all_gather | solution.py:200
  231.6 3.3 copy.174
  234.9 1.4 gather_fusion.1
  236.3 65.2 %all-gather.19.cloned.1.call-done = bf16[4096,1,256]{2,0,1:T(8,128)(2,1)} async-done(((bf16[128,1,256]{2,0,1:T(8,128)(2,1)}), bf16[4096,1,256]{2,0,1:T(8,128)(2,1)}) %all-gather.19.cloned.1.call-update) | async-done | bytes 2097168 | tf_op jit(solution)/shard_map/all_gather | solution.py:199
  301.5 2.3 gather_fusion
  308.2 65.6 %all-gather.25.cloned.1.call-done = f32[64,128,128]{2,1,0:T(8,128)} async-done(((f32[2,128,128]{2,1,0:T(8,128)}), f32[64,128,128]{2,1,0:T(8,128)}) %all-gather.25.cloned.1.call-update) | async-done | bytes 4194320 | tf_op jit(solution)/shard_map/all_gather | solution.py:18
  373.9 5.6 copy.184
  379.5 4.6 rev.7
  384.1 62.6 %all-gather.23.cloned.1.call-done = f32[64,128,128]{2,1,0:T(8,128)} async-done(((f32[2,128,128]{2,1,0:T(8,128)}), f32[64,128,128]{2,1,0:T(8,128)}) %all-gather.23.cloned.1.call-update) | async-done | bytes 4194320 | tf_op jit(solution)/shard_map/all_gather | solution.py:18
  446.7 5.6 copy.180
  452.3 4.7 rev.6
  456.9 40.1 %while.175 = (s32[]{:T(128)}, f32[2,128,128]{1,2,0:T(8,128)S(1)}, s32[]{:T(128)}, f32[32,2,128,128]{2,3,1,0:T(8,128)}, f32[32,2,128,128]{2,3,1,0:T(8,128)}, /*index=5*/s32[]{:T(128)}, s32[]{:T(128)}) while((s32[]{:T(128)}, f32[2,128,128]{1,2,0:T(8,128)S(1)}, s32[]{:T(128)}, f32[32,2,128,128]{2,3,1,0:T(8,128)}, ...), condition=%wide.region_15.18_spmd.clone, body=%wide.region_14.17_spmd.clone.sunk | while | flops 50462724 | bytes 920159 | solution.py:30
  497.2 21.8 %all-gather.29.cloned.1.call-done = f32[64,128,128]{2,1,0:T(8,128)} async-done(((f32[2,128,128]{2,1,0:T(8,128)}), f32[64,128,128]{2,1,0:T(8,128)}) %all-gather.29.cloned.1.call-update) | async-done | bytes 4194320 | tf_op jit(solution)/shard_map/all_gather | solution.py:18
  519.0 72.6 %all-gather.27.cloned.1.call-done = f32[64,128,128]{2,1,0:T(8,128)} async-done(((f32[2,128,128]{2,1,0:T(8,128)}), f32[64,128,128]{2,1,0:T(8,128)}) %all-gather.27.cloned.1.call-update) | async-done | bytes 4194320 | tf_op jit(solution)/shard_map/all_gather | solution.py:18
  591.6 73.7 %while.176 = (s32[]{:T(128)}, f32[2,128,128]{1,2,0:T(8,128)S(1)}, s32[]{:T(128)}, f32[32,2,128,128]{3,2,1,0:T(8,128)}, f32[32,2,128,128]{3,2,1,0:T(8,128)}, /*index=5*/s32[]{:T(128)}, s32[]{:T(128)}) while((s32[]{:T(128)}, f32[2,128,128]{1,2,0:T(8,128)S(1)}, s32[]{:T(128)}, f32[32,2,128,128]{3,2,1,0:T(8,128)}, ...), condition=%wide.region_17.20_spmd.clone, body=%wide.region_16.19_spmd.clone.sunk | while | flops 50462724 | bytes 1443939 | solution.py:30
  606.9 1.3 fusion.512
  611.7 1.3 fusion.512
  635.5 1.3 fusion.512
  640.2 1.3 fusion.512
  642.6 1.3 fusion.512
  664.0 1.3 fusion.512
  666.0 28.2 %while.172 = (s32[]{:T(128)}, f32[2,128,128]{2,1,0:T(8,128)S(1)}, f32[2,2,64,64]{3,2,1,0:T(8,128)S(1)}, f32[2,2,64,64]{3,2,1,0:T(8,128)S(1)}, f32[2,2,64,64]{3,2...) while((s32[]{:T(128)}, f32[2,128,128]{2,1,0:T(8,128)S(1)}, ...), condition=%wide.region_20.23_spmd.clone.clone, body=%wide.region_18.22_spmd.clone.clone.sunk | while | flops 113643840 | bytes 2896269 | solution.py:90
  667.4 9.8 %custom-call.44 = f32[2,1,64,64]{2,3,1,0:T(8,128)S(1)} custom-call(f32[2,1,64,64]{3,2,1,0:T(8,128)S(1)} %add_bitcast_fusion.6), custom_call_target="InvertDiagBlocksLowerTriangular" | custom-call | tf_op jit(solution)/shard_map/jvp()/while/body/eval_jaxpr/triangular_solve/custom-call.1 | solution.py:52
  681.4 9.8 %custom-call.44 = f32[2,1,64,64]{2,3,1,0:T(8,128)S(1)} custom-call(f32[2,1,64,64]{3,2,1,0:T(8,128)S(1)} %add_bitcast_fusion.6), custom_call_target="InvertDiagBlocksLowerTriangular" | custom-call | tf_op jit(solution)/shard_map/jvp()/while/body/eval_jaxpr/triangular_solve/custom-call.1 | solution.py:52
  694.3 54.4 %while.173 = (s32[]{:T(128)}, f32[2,128,128]{2,1,0:T(8,128)S(1)}, f32[2,2,64,128]{3,2,1,0:T(8,128)S(1)}, f32[2,2,64,128]{3,2,1,0:T(8,128)S(1)}, f32[2,2,64,128]{...) while((s32[]{:T(128)}, f32[2,128,128]{2,1,0:T(8,128)S(1)}, ...), condition=%wide.region_32.35_spmd.clone.clone, body=%wide.region_21.34_spmd.clone.clone.sunk | while | flops 258757312 | bytes 5322969 | solution.py:90
  695.7 9.8 %custom-call.46 = f32[2,1,64,64]{2,3,1,0:T(8,128)S(1)} custom-call(f32[2,1,64,64]{3,2,1,0:T(8,128)S(1)} %add_bitcast_fusion.7), custom_call_target="InvertDiagBlocksLowerTriangular" | custom-call | tf_op jit(solution)/shard_map/transpose(jvp())/while/body/eval_jaxpr/triangular_solve | solution.py:52
  706.0 9.8 %custom-call.45 = f32[2,1,64,64]{2,3,1,0:T(8,128)S(1)} custom-call(f32[2,1,64,64]{3,2,1,0:T(8,128)S(1)} %fusion.479), custom_call_target="InvertDiagBlocksLowerTriangular" | custom-call | tf_op jit(solution)/shard_map/transpose(jvp())/while/body/eval_jaxpr/triangular_solve/custom-call.0 | solution.py:52
  722.9 9.8 %custom-call.46 = f32[2,1,64,64]{2,3,1,0:T(8,128)S(1)} custom-call(f32[2,1,64,64]{3,2,1,0:T(8,128)S(1)} %add_bitcast_fusion.7), custom_call_target="InvertDiagBlocksLowerTriangular" | custom-call | tf_op jit(solution)/shard_map/transpose(jvp())/while/body/eval_jaxpr/triangular_solve | solution.py:52
  733.2 9.8 %custom-call.45 = f32[2,1,64,64]{2,3,1,0:T(8,128)S(1)} custom-call(f32[2,1,64,64]{3,2,1,0:T(8,128)S(1)} %fusion.479), custom_call_target="InvertDiagBlocksLowerTriangular" | custom-call | tf_op jit(solution)/shard_map/transpose(jvp())/while/body/eval_jaxpr/triangular_solve/custom-call.0 | solution.py:52
  749.7 1.3 fusion.302
  751.1 1.3 fusion.299
  754.7 1.3 add_add_fusion
  756.0 1.4 add_add_fusion.1
  757.4 1.7 copy.420
  759.1 1.7 copy.421
  (584 shorter events, 171.7 us)
Async XLA Ops:
  7.2 95.0 %all-gather.15.cloned.1.call-start = ((), (), s32[]{:S(2)}) async-start(), calls=%async_computation | async-start | bytes 2162688 | tf_op jit(solution)/shard_map/all_gather | solution.py:226
  7.9 151.0 %all-gather.17.cloned.1.call-start = ((), (), s32[]{:S(2)}) async-start(), calls=%async_computation.1 | async-start | bytes 2162688 | tf_op jit(solution)/shard_map/all_gather | solution.py:229
  8.7 223.0 %all-gather.21.cloned.1.call-start = ((), (), s32[]{:S(2)}) async-start(), calls=%async_computation.3 | async-start | bytes 2162688 | tf_op jit(solution)/shard_map/all_gather | solution.py:200
  10.4 291.1 %all-gather.19.cloned.1.call-start = ((), (), s32[]{:S(2)}) async-start(), calls=%async_computation.2 | async-start | bytes 2162688 | tf_op jit(solution)/shard_map/all_gather | solution.py:199
  12.2 361.7 %all-gather.25.cloned.1.call-start = ((), (), s32[]{:S(2)}) async-start(), calls=%async_computation.5 | async-start | bytes 4325376 | tf_op jit(solution)/shard_map/all_gather | solution.py:18
  13.2 1.4 copy-start.28
  13.8 3.2 copy-start.23
  15.5 0.6 copy-start.27
  16.1 1.5 copy-start.24
  17.6 0.8 copy-start.25
  20.4 24.5 %copy-start.19 = (bf16[128,256]{1,0:T(8,128)(2,1)S(1)}, bf16[128,256]{1,0:T(8,128)(2,1)}, u32[]{:S(2)}) copy-start(bf16[128,256]{1,0:T(8,128)(2,1)} %param.47) | copy-start | bytes 196612
  44.8 0.7 copy-start.2
  69.0 0.6 copy-start.1
  69.7 377.0 %all-gather.23.cloned.1.call-start = ((), (), s32[]{:S(2)}) async-start(), calls=%async_computation.4 | async-start | bytes 4325376 | tf_op jit(solution)/shard_map/all_gather | solution.py:18
  69.8 26.5 %copy-start.5 = (bf16[128,1,256]{0,2,1:T(8,128)(2,1)S(1)}, bf16[128,1,256]{0,2,1:T(8,128)(2,1)}, u32[]{:S(2)}) copy-start(bf16[128,1,256]{0,2,1:T(8,128)(2,1)} %constant_dynamic-slice_fusion.18) | copy-start | bytes 196612
  69.8 26.6 %copy-start.21 = (s32[1,64,4]{1,2,0:T(4,128)S(1)}, s32[1,64,4]{1,2,0:T(4,128)}, u32[]{:S(2)}) copy-start(s32[1,64,4]{1,2,0:T(4,128)} %param.39) | copy-start | bytes 3076
  69.8 27.8 %copy-start.31 = (f32[1,4096]{1,0:T(1,128)S(1)}, f32[1,4096]{1,0:T(1,128)}, u32[]{:S(2)}) copy-start(f32[1,4096]{1,0:T(1,128)} %param.37) | copy-start | bytes 49156
  69.8 27.9 %copy-start.20 = (f32[1,4096]{1,0:T(1,128)S(1)}, f32[1,4096]{1,0:T(1,128)}, u32[]{:S(2)}) copy-start(f32[1,4096]{1,0:T(1,128)} %param.38) | copy-start | bytes 49156
  69.8 31.3 %copy-start.6 = (bf16[128,1,256]{2,0,1:T(8,128)(2,1)S(1)}, bf16[128,1,256]{2,0,1:T(8,128)(2,1)}, u32[]{:S(2)}) copy-start(bf16[128,1,256]{2,0,1:T(8,128)(2,1)} %copy.214) | copy-start | bytes 196612
  69.9 31.3 %copy-start.15 = (bf16[128,256]{1,0:T(8,128)(2,1)S(1)}, bf16[128,256]{1,0:T(8,128)(2,1)}, u32[]{:S(2)}) copy-start(bf16[128,256]{1,0:T(8,128)(2,1)} %param.33) | copy-start | bytes 196612
  69.9 31.5 %copy-start.8 = (bf16[128,256]{1,0:T(8,128)(2,1)S(1)}, bf16[128,256]{1,0:T(8,128)(2,1)}, u32[]{:S(2)}) copy-start(bf16[128,256]{1,0:T(8,128)(2,1)} %param.36) | copy-start | bytes 196612
  93.6 1.6 copy-start
  93.6 2.3 copy-start.12
  93.6 2.3 copy-start.17
  94.4 424.6 %all-gather.29.cloned.1.call-start = ((), (), s32[]{:S(2)}) async-start(), calls=%async_computation.7 | async-start | bytes 4325376 | tf_op jit(solution)/shard_map/all_gather | solution.py:18
  95.2 496.5 %all-gather.27.cloned.1.call-start = ((), (), s32[]{:S(2)}) async-start(), calls=%async_computation.6 | async-start | bytes 4325376 | tf_op jit(solution)/shard_map/all_gather | solution.py:18
  95.9 661.5 %all-reduce.5.cloned.1.call-start = ((), (), s32[]{:S(2)}) async-start(), calls=%async_computation.8 | async-start | bytes 1048576 | tf_op jit(solution)/shard_map/psum | solution.py:252
  97.7 4.4 copy-start.26
  97.8 4.3 copy-start.22
  158.9 2.6 copy-start.4
  161.5 1.6 copy-start.3
  165.2 139.7 %copy-start.9 = (bf16[128,256]{1,0:T(8,128)(2,1)S(1)}, bf16[128,256]{1,0:T(8,128)(2,1)}, u32[]{:S(2)}) copy-start(bf16[128,256]{1,0:T(8,128)(2,1)} %param.36) | copy-start | bytes 196612
  236.3 70.2 %copy-start.16 = (f32[2,64,64]{1,2,0:T(8,128)S(1)}, f32[2,64,64]{1,2,0:T(8,128)}, u32[]{:S(2)}) copy-start(f32[2,64,64]{1,2,0:T(8,128)} %fusion.283) | copy-start | bytes 98308
  236.3 71.1 %copy-start.7 = (f32[16,8,2,256]{3,1,2,0:T(8,128)S(1)}, f32[16,8,2,256]{3,1,2,0:T(8,128)}, u32[]{:S(2)}) copy-start(f32[16,8,2,256]{3,1,2,0:T(8,128)} %copy.217) | copy-start | bytes 786436
  236.3 71.1 %copy-start.30 = (pred[512]{0:T(512)(128)(4,1)S(1)}, pred[512]{0:T(512)(128)(4,1)}, u32[]{:S(2)}) copy-start(pred[512]{0:T(512)(128)(4,1)} %broadcast_in_dim.479) | copy-start | bytes 1540
  665.3 0.7 copy-start.13
  665.3 0.7 copy-start.18
  666.0 28.2 %copy-start.14 = (pred[64,64]{1,0:T(8,128)(4,1)S(1)}, pred[64,64]{1,0:T(8,128)(4,1)}, u32[]{:S(2)}) copy-start(pred[64,64]{1,0:T(8,128)(4,1)} %iota_compare_fusion.16) | copy-start | bytes 12292
  694.2 54.5 %copy-start.10 = (bf16[128,128]{1,0:T(8,128)(2,1)S(1)}, bf16[128,128]{1,0:T(8,128)(2,1)}, u32[]{:S(2)}) copy-start(bf16[128,128]{1,0:T(8,128)(2,1)} %param.41) | copy-start | bytes 98308
  694.3 55.3 %copy-start.29 = (f32[128]{0:T(128)S(1)}, f32[128]{0:T(128)}, u32[]{:S(2)}) copy-start(f32[128]{0:T(128)} %copy-done.28) | copy-start | bytes 1540
  694.3 58.2 %copy-start.11 = (bf16[128,128]{1,0:T(8,128)(2,1)S(1)}, bf16[128,128]{1,0:T(8,128)(2,1)}, u32[]{:S(2)}) copy-start(bf16[128,128]{1,0:T(8,128)(2,1)} %param.40) | copy-start | bytes 98308
  694.3 22.1 %copy-start.32 = (f32[2,2,1,1]{1,3,2,0:T(1,128)}, f32[2,2,1,1]{1,3,2,0:T(1,128)S(1)}, u32[]{:S(2)}) copy-start(f32[2,2,1,1]{1,3,2,0:T(1,128)S(1)} %get-tuple-element.4409) | copy-start | bytes 52 | tf_op jit(solution)/shard_map/transpose(jvp())/while
  717.5 4.0 copy-start.33
  721.5 22.1 %copy-start.32 = (f32[2,2,1,1]{1,3,2,0:T(1,128)}, f32[2,2,1,1]{1,3,2,0:T(1,128)S(1)}, u32[]{:S(2)}) copy-start(f32[2,2,1,1]{1,3,2,0:T(1,128)S(1)} %get-tuple-element.4409) | copy-start | bytes 52 | tf_op jit(solution)/shard_map/transpose(jvp())/while
  744.7 4.0 copy-start.33
Sparse Core Ops, SparseCore 0:
  10.1 79.2 all-gather.14
  91.5 67.3 all-gather.16
  161.5 70.0 all-gather.20
  234.2 67.3 all-gather.18
  303.5 70.3 all-gather.24
  376.4 70.1 all-gather.22
  448.8 70.1 all-gather.28
  521.1 70.4 all-gather.26
  595.5 111.3 all-reduce.4
where the time goes:
time: 770 us; the launch traced here: 767 us
  waiting for transfers between devices  411 us (53%)
  other arithmetic  142 us (18%)
  matrix products  114 us (15%)
  local copies, waits for them, and re-layouts  80.6 us (10%)
  between operations  14.9 us (2%)
    all_gather x4, waiting for transfers between devices, prefix(): pieces = jax.tree.map(lambda part: lax.all_gather(part, axis), value)  223 us
    another operation x44, other arithmetic, span_update(): lax.linalg.triangular_solve(system, target, left_side=True, lower=True, u...  119 us
    dot_general x62, matrix products, compose_maps(): jnp.einsum('hij,hjk->hik', earlier[1], later[0], precision=HIGHEST)  79.1 us
    all_gather x1, waiting for transfers between devices, on_device(): lax.all_gather(own_values, 'ctx', axis=0, tiled=True)  66.4 us
    all_gather x1, waiting for transfers between devices, on_device(): lax.all_gather(own_keys, 'ctx', axis=0, tiled=True)  65.2 us
    all_gather x1, waiting for transfers between devices, on_device(): lax.all_gather(attn_cot, 'ctx', axis=0, tiled=True)  53.9 us
    dynamic_slice x62, local copies, waits for them, and re-layouts, turn(): longer = join(so_far, jax.tree.map(lambda part: part[position], pieces))  31.4 us
  transfers between devices with their start and end apart: 9, of which 7 were waited for; matrix products, arithmetic and copies ran while one was open for 43% of the time, Pallas kernels for 0%

commit v1 on v0

--- a/solution.py
+++ b/solution.py
@@ -195,8 +195,19 @@
     member_rows = jnp.repeat(jnp.repeat(member, BLK, axis=1), BLK, axis=2)
     key_pos = row_base + jnp.arange(tok_rows, dtype=jnp.int32)
     key_block = key_pos // BLK
+
+    def launch_the_sums_all(own_rows, across):
+        o_now = lax.all_to_all(
+            jnp.stack([own_rows for _ in range(lax.axis_size(across))]),
+            across,
+            split_axis=0,
+            concat_axis=0,
+        )
+        w1 = jnp.concatenate(o_now, 0)
+        return w1
+
     keys_whole, values_whole = (
-        lax.all_gather(own_keys, "ctx", axis=0, tiled=True),
+        launch_the_sums_all(own_keys, "ctx"),
         lax.all_gather(own_values, "ctx", axis=0, tiled=True),
     )
     lists_own = lax.dynamic_slice_in_dim(block_lists, first_block, blocks_here, 1)

time: 770 us -> 738 us (0.958)
  waiting for transfers between devices: 411 us -> 360 us
  starting transfers between devices: 0.54 us -> 17.4 us
    all_gather x1 -> x0, waiting for transfers between devices: 65.2 us -> none  [on_device(): lax.all_gather(own_keys, 'ctx', axis=0, tiled=True)]
    all_to_all x0 -> x1, starting transfers between devices: none -> 16.9 us  [launch_the_sums_all(): lax.all_to_all(jnp.stack([own_rows for _ in range(lax.axis_size(across))]...]
    all_gather x1, waiting for transfers between devices: 53.9 us -> 64.4 us  [on_device(): lax.all_gather(attn_cot, 'ctx', axis=0, tiled=True)]
  transfers between devices with their start and end apart: 9 -> 9, of which waited for: 7 -> 6; matrix products, arithmetic and copies ran while one was open for 43% -> 45% of each run, Pallas kernels for 0% -> 0%
where the time goes in v1:
time: 738 us; the launch traced here: 735 us
  waiting for transfers between devices  360 us (49%)
  other arithmetic  144 us (20%)
  matrix products  115 us (16%)
  local copies, waits for them, and re-layouts  79.6 us (11%)
  starting transfers between devices  17.4 us (2%)
  between operations  15.1 us (2%)
    all_gather x4, waiting for transfers between devices, prefix(): pieces = jax.tree.map(lambda part: lax.all_gather(part, axis), value)  224 us
    another operation x44, other arithmetic, span_update(): lax.linalg.triangular_solve(system, target, left_side=True, lower=True, u...  119 us
    dot_general x62, matrix products, compose_maps(): jnp.einsum('hij,hjk->hik', earlier[1], later[0], precision=HIGHEST)  79.2 us
    all_gather x1, waiting for transfers between devices, on_device(): lax.all_gather(own_values, 'ctx', axis=0, tiled=True)  69 us
    all_gather x1, waiting for transfers between devices, on_device(): lax.all_gather(attn_cot, 'ctx', axis=0, tiled=True)  64.4 us
    dynamic_slice x62, local copies, waits for them, and re-layouts, turn(): longer = join(so_far, jax.tree.map(lambda part: part[position], pieces))  31.4 us
    all_to_all x1, starting transfers between devices, launch_the_sums_all(): lax.all_to_all(jnp.stack([own_rows for _ in range(lax.axis_size(across))]...  16.9 us
  transfers between devices with their start and end apart: 9, of which 6 were waited for; matrix products, arithmetic and copies ran while one was open for 45% of the time, Pallas kernels for 0%

profile of v1, /device:TPU:1, one launch (start us, length us, event | category | flops | bytes accessed | tf_op | source)
XLA Modules:
  0.0 735.0 jit_solution(5084858875441547665)
XLA Ops:
  19.2 24.4 %while.177 = (s32[]{:T(128)}, f32[2,128,128]{2,1,0:T(8,128)S(1)}, f32[2,2,64,1]{2,1,3,0:T(2,128)S(1)}, f32[2,2,64,1]{2,1,3,0:T(2,128)S(1)}, f32[2,2,64,64]{3,2,1...) while((s32[]{:T(128)}, f32[2,128,128]{2,1,0:T(8,128)S(1)}, ...), condition=%wide.region_11.13_spmd.clone.clone, body=%wide.region_9.12_spmd.clone.clone.sunk | while | flops 88404160 | bytes 1473784 | solution.py:90
  20.5 9.8 %custom-call.48 = f32[2,1,64,64]{2,3,1,0:T(8,128)S(1)} custom-call(f32[2,1,64,64]{3,2,1,0:T(8,128)S(1)} %add_bitcast_fusion.8), custom_call_target="InvertDiagBlocksLowerTriangular" | custom-call | tf_op jit(solution)/shard_map/jvp()/while/body/eval_jaxpr/triangular_solve/custom-call.1 | solution.py:52
  32.7 9.8 %custom-call.48 = f32[2,1,64,64]{2,3,1,0:T(8,128)S(1)} custom-call(f32[2,1,64,64]{3,2,1,0:T(8,128)S(1)} %add_bitcast_fusion.8), custom_call_target="InvertDiagBlocksLowerTriangular" | custom-call | tf_op jit(solution)/shard_map/jvp()/while/body/eval_jaxpr/triangular_solve/custom-call.1 | solution.py:52
  44.3 23.5 %while.174 = (s32[]{:T(128)}, f32[2,128,128]{2,1,0:T(8,128)S(1)}, f32[2,2,1,1]{1,3,2,0:T(1,128)S(1)}, f32[2,2,64,1]{2,1,3,0:T(2,128)S(1)}, f32[2,2,64,128]{3,2,1...) while((s32[]{:T(128)}, f32[2,128,128]{2,1,0:T(8,128)S(1)}, ...), condition=%wide.region_13.16_spmd.clone, body=%wide.region_12.15_spmd.clone.sunk | while | flops 100954176 | bytes 1590971 | solution.py:90
  45.1 9.8 %custom-call.47 = f32[2,1,64,64]{2,3,1,0:T(8,128)S(1)} custom-call(f32[2,1,64,64]{3,2,1,0:T(8,128)S(1)} %fusion.505), custom_call_target="InvertDiagBlocksLowerTriangular" | custom-call | tf_op jit(solution)/shard_map/transpose(jvp())/while/body/eval_jaxpr/triangular_solve/custom-call.0 | solution.py:52
  56.9 9.8 %custom-call.47 = f32[2,1,64,64]{2,3,1,0:T(8,128)S(1)} custom-call(f32[2,1,64,64]{3,2,1,0:T(8,128)S(1)} %fusion.505), custom_call_target="InvertDiagBlocksLowerTriangular" | custom-call | tf_op jit(solution)/shard_map/transpose(jvp())/while/body/eval_jaxpr/triangular_solve/custom-call.0 | solution.py:52
  68.6 23.7 %while.171 = (s32[]{:T(128)}, f32[2,128,128]{2,1,0:T(8,128)S(1)}, f32[2,2,64]{2,1,0:T(2,128)S(1)}, f32[2,2,64]{2,1,0:T(2,128)S(1)}, f32[2,2,64,128]{3,2,1,0:T(8,128)S(1)}, /*index=5*/s32[]{:T(128)}, f32[]{:T(128)}) while((s32[]{:T(128)}, f32[2,128,128]{2,1,0:T(8,128)S(1)}, f32[2,2,64]{2,1,0:T(2,128)S(1)}, f32[2,2,64]{2,1,0:T(2,128)S(1)}, ...), condition=%wide.region_7.9_spmd, body=%wide.region_5.8_spmd.sunk | while | flops 75726912 | bytes 1051785 | solution.py:90
  69.9 9.9 %custom-call.43 = f32[2,1,64,64]{2,3,1,0:T(8,128)S(1)} custom-call(f32[2,1,64,64]{3,2,1,0:T(8,128)S(1)} %fusion.440), custom_call_target="InvertDiagBlocksLowerTriangular" | custom-call | tf_op jit(solution)/shard_map/while/body/eval_jaxpr/triangular_solve/custom-call.1 | solution.py:52
  81.7 9.8 %custom-call.43 = f32[2,1,64,64]{2,3,1,0:T(8,128)S(1)} custom-call(f32[2,1,64,64]{3,2,1,0:T(8,128)S(1)} %fusion.440), custom_call_target="InvertDiagBlocksLowerTriangular" | custom-call | tf_op jit(solution)/shard_map/while/body/eval_jaxpr/triangular_solve/custom-call.1 | solution.py:52
  94.7 1.6 stack.5
  96.3 16.9 %all-to-all-start = ((bf16[32,128,256]{2,1,0:T(8,128)(2,1)}), bf16[32,128,256]{2,1,0:T(8,128)(2,1)}, u32[]{:S(2)}, u32[]{:S(2)}) async-start(bf16[32,128,256]{2,1,0:T(8,128)(2,1)} %stack.5), calls=%async_computation | async-start | bytes 4194304 | tf_op jit(solution)/shard_map/all_to_all | solution.py:200
  121.3 3.0 fusion.267
  124.3 64.4 %all-gather.15.cloned.1.call-done = bf16[4096,256]{1,0:T(8,128)(2,1)} async-done(((bf16[128,256]{1,0:T(8,128)(2,1)}), bf16[4096,256]{1,0:T(8,128)(2,1)}) %all-gather.15.cloned.1.call-update) | async-done | bytes 2097168 | tf_op jit(solution)/shard_map/all_gather | solution.py:240
  188.7 2.6 fusion.271
  191.3 1.3 convolution_multiply_fusion.11
  194.9 69.0 %all-gather.17.cloned.1.call-done = bf16[4096,1,256]{0,2,1:T(8,128)(2,1)} async-done(((bf16[128,1,256]{0,2,1:T(8,128)(2,1)}), bf16[4096,1,256]{0,2,1:T(8,128)(2,1)}) %all-gather.17.cloned.1.call-update) | async-done | bytes 2097168 | tf_op jit(solution)/shard_map/all_gather | solution.py:211
  263.9 3.3 copy.174
  267.2 1.4 gather_fusion.1
  268.6 1.8 broadcast_select_fusion
  270.4 67.2 %all-gather.21.cloned.1.call-done = f32[64,128,128]{2,1,0:T(8,128)} async-done(((f32[2,128,128]{2,1,0:T(8,128)}), f32[64,128,128]{2,1,0:T(8,128)}) %all-gather.21.cloned.1.call-update) | async-done | bytes 4194320 | tf_op jit(solution)/shard_map/all_gather | solution.py:18
  337.7 5.6 copy.184
  343.3 4.6 rev.7
  347.9 62.5 %all-gather.19.cloned.1.call-done = f32[64,128,128]{2,1,0:T(8,128)} async-done(((f32[2,128,128]{2,1,0:T(8,128)}), f32[64,128,128]{2,1,0:T(8,128)}) %all-gather.19.cloned.1.call-update) | async-done | bytes 4194320 | tf_op jit(solution)/shard_map/all_gather | solution.py:18
  410.4 5.6 copy.180
  416.0 4.7 rev.6
  420.7 40.2 %while.175 = (s32[]{:T(128)}, f32[2,128,128]{1,2,0:T(8,128)S(1)}, s32[]{:T(128)}, f32[32,2,128,128]{2,3,1,0:T(8,128)}, f32[32,2,128,128]{2,3,1,0:T(8,128)}, /*index=5*/s32[]{:T(128)}, s32[]{:T(128)}) while((s32[]{:T(128)}, f32[2,128,128]{1,2,0:T(8,128)S(1)}, s32[]{:T(128)}, f32[32,2,128,128]{2,3,1,0:T(8,128)}, ...), condition=%wide.region_15.18_spmd.clone, body=%wide.region_14.17_spmd.clone.sunk | while | flops 50462724 | bytes 920159 | solution.py:30
  424.6 1.3 fusion.509
  461.0 22.2 %all-gather.25.cloned.1.call-done = f32[64,128,128]{2,1,0:T(8,128)} async-done(((f32[2,128,128]{2,1,0:T(8,128)}), f32[64,128,128]{2,1,0:T(8,128)}) %all-gather.25.cloned.1.call-update) | async-done | bytes 4194320 | tf_op jit(solution)/shard_map/all_gather | solution.py:18
  483.2 71.9 %all-gather.23.cloned.1.call-done = f32[64,128,128]{2,1,0:T(8,128)} async-done(((f32[2,128,128]{2,1,0:T(8,128)}), f32[64,128,128]{2,1,0:T(8,128)}) %all-gather.23.cloned.1.call-update) | async-done | bytes 4194320 | tf_op jit(solution)/shard_map/all_gather | solution.py:18
  555.1 73.7 %while.176 = (s32[]{:T(128)}, f32[2,128,128]{1,2,0:T(8,128)S(1)}, s32[]{:T(128)}, f32[32,2,128,128]{3,2,1,0:T(8,128)}, f32[32,2,128,128]{3,2,1,0:T(8,128)}, /*index=5*/s32[]{:T(128)}, s32[]{:T(128)}) while((s32[]{:T(128)}, f32[2,128,128]{1,2,0:T(8,128)S(1)}, s32[]{:T(128)}, f32[32,2,128,128]{3,2,1,0:T(8,128)}, ...), condition=%wide.region_17.20_spmd.clone, body=%wide.region_16.19_spmd.clone.sunk | while | flops 50462724 | bytes 1443939 | solution.py:30
  570.4 1.3 fusion.512
  575.1 1.3 fusion.512
  598.9 1.3 fusion.512
  627.4 1.3 fusion.512
  629.5 25.9 %while.172 = (s32[]{:T(128)}, f32[2,128,128]{2,1,0:T(8,128)S(1)}, f32[2,2,64,64]{3,2,1,0:T(8,128)S(1)}, f32[2,2,64,64]{3,2,1,0:T(8,128)S(1)}, f32[2,2,64,64]{3,2...) while((s32[]{:T(128)}, f32[2,128,128]{2,1,0:T(8,128)S(1)}, ...), condition=%wide.region_20.23_spmd.clone.clone, body=%wide.region_18.22_spmd.clone.clone.sunk | while | flops 113643840 | bytes 2896269 | solution.py:90
  630.8 9.8 %custom-call.44 = f32[2,1,64,64]{2,3,1,0:T(8,128)S(1)} custom-call(f32[2,1,64,64]{3,2,1,0:T(8,128)S(1)} %add_bitcast_fusion.6), custom_call_target="InvertDiagBlocksLowerTriangular" | custom-call | tf_op jit(solution)/shard_map/jvp()/while/body/eval_jaxpr/triangular_solve/custom-call.1 | solution.py:52
  643.8 9.8 %custom-call.44 = f32[2,1,64,64]{2,3,1,0:T(8,128)S(1)} custom-call(f32[2,1,64,64]{3,2,1,0:T(8,128)S(1)} %add_bitcast_fusion.6), custom_call_target="InvertDiagBlocksLowerTriangular" | custom-call | tf_op jit(solution)/shard_map/jvp()/while/body/eval_jaxpr/triangular_solve/custom-call.1 | solution.py:52
  656.1 54.4 %while.173 = (s32[]{:T(128)}, f32[2,128,128]{2,1,0:T(8,128)S(1)}, f32[2,2,64,128]{3,2,1,0:T(8,128)S(1)}, f32[2,2,64,128]{3,2,1,0:T(8,128)S(1)}, f32[2,2,64,128]{...) while((s32[]{:T(128)}, f32[2,128,128]{2,1,0:T(8,128)S(1)}, ...), condition=%wide.region_32.35_spmd.clone.clone, body=%wide.region_21.34_spmd.clone.clone.sunk | while | flops 258757312 | bytes 5289689 | solution.py:90
  657.5 9.8 %custom-call.46 = f32[2,1,64,64]{2,3,1,0:T(8,128)S(1)} custom-call(f32[2,1,64,64]{3,2,1,0:T(8,128)S(1)} %add_bitcast_fusion.7), custom_call_target="InvertDiagBlocksLowerTriangular" | custom-call | tf_op jit(solution)/shard_map/transpose(jvp())/while/body/eval_jaxpr/triangular_solve | solution.py:52
  667.8 9.8 %custom-call.45 = f32[2,1,64,64]{2,3,1,0:T(8,128)S(1)} custom-call(f32[2,1,64,64]{3,2,1,0:T(8,128)S(1)} %fusion.479), custom_call_target="InvertDiagBlocksLowerTriangular" | custom-call | tf_op jit(solution)/shard_map/transpose(jvp())/while/body/eval_jaxpr/triangular_solve/custom-call.0 | solution.py:52
  684.7 9.8 %custom-call.46 = f32[2,1,64,64]{2,3,1,0:T(8,128)S(1)} custom-call(f32[2,1,64,64]{3,2,1,0:T(8,128)S(1)} %add_bitcast_fusion.7), custom_call_target="InvertDiagBlocksLowerTriangular" | custom-call | tf_op jit(solution)/shard_map/transpose(jvp())/while/body/eval_jaxpr/triangular_solve | solution.py:52
  695.0 9.8 %custom-call.45 = f32[2,1,64,64]{2,3,1,0:T(8,128)S(1)} custom-call(f32[2,1,64,64]{3,2,1,0:T(8,128)S(1)} %fusion.479), custom_call_target="InvertDiagBlocksLowerTriangular" | custom-call | tf_op jit(solution)/shard_map/transpose(jvp())/while/body/eval_jaxpr/triangular_solve/custom-call.0 | solution.py:52
  713.7 1.3 fusion.301
  715.1 1.3 fusion.298
  716.4 1.4 add_add_fusion
  717.8 2.3 gather_fusion
  724.8 1.7 copy.422
  726.5 1.7 copy.423
  (587 shorter events, 172.4 us)
Async XLA Ops:
  7.2 114.2 %all-gather.13.cloned.1.call-start = ((), (), s32[]{:S(2)}) async-start(), calls=%async_computation.1 | async-start | bytes 2162688 | tf_op jit(solution)/shard_map/all_gather | solution.py:237
  7.9 180.8 %all-gather.15.cloned.1.call-start = ((), (), s32[]{:S(2)}) async-start(), calls=%async_computation.2 | async-start | bytes 2162688 | tf_op jit(solution)/shard_map/all_gather | solution.py:240
  8.7 255.3 %all-gather.17.cloned.1.call-start = ((), (), s32[]{:S(2)}) async-start(), calls=%async_computation.3 | async-start | bytes 2162688 | tf_op jit(solution)/shard_map/all_gather | solution.py:211
  10.4 327.2 %all-gather.21.cloned.1.call-start = ((), (), s32[]{:S(2)}) async-start(), calls=%async_computation.5 | async-start | bytes 4325376 | tf_op jit(solution)/shard_map/all_gather | solution.py:18
  11.4 2.9 copy-start.29
  12.0 0.9 copy-start.26
  13.7 3.5 copy-start.30
  14.3 0.9 copy-start.24
  15.8 0.6 copy-start.27
  19.2 24.4 %copy-start.19 = (bf16[128,256]{1,0:T(8,128)(2,1)S(1)}, bf16[128,256]{1,0:T(8,128)(2,1)}, u32[]{:S(2)}) copy-start(bf16[128,256]{1,0:T(8,128)(2,1)} %param.47) | copy-start | bytes 196612
  43.6 0.6 copy-start.2
  67.8 0.7 copy-start.1
  68.5 341.9 %all-gather.19.cloned.1.call-start = ((), (), s32[]{:S(2)}) async-start(), calls=%async_computation.4 | async-start | bytes 4325376 | tf_op jit(solution)/shard_map/all_gather | solution.py:18
  68.6 25.9 %copy-start.18 = (bf16[128,512]{1,0:T(8,128)(2,1)S(1)}, bf16[128,512]{1,0:T(8,128)(2,1)}, u32[]{:S(2)}) copy-start(bf16[128,512]{1,0:T(8,128)(2,1)} %param.34) | copy-start | bytes 393220
  92.3 1.4 copy-start
  92.3 3.9 copy-start.11
  92.3 3.9 copy-start.16
  93.1 390.1 %all-gather.25.cloned.1.call-start = ((), (), s32[]{:S(2)}) async-start(), calls=%async_computation.7 | async-start | bytes 4325376 | tf_op jit(solution)/shard_map/all_gather | solution.py:18
  93.7 461.4 %all-gather.23.cloned.1.call-start = ((), (), s32[]{:S(2)}) async-start(), calls=%async_computation.6 | async-start | bytes 4325376 | tf_op jit(solution)/shard_map/all_gather | solution.py:18
  96.2 17.4 %copy-start.5 = (bf16[128,1,256]{0,2,1:T(8,128)(2,1)S(1)}, bf16[128,1,256]{0,2,1:T(8,128)(2,1)}, u32[]{:S(2)}) copy-start(bf16[128,1,256]{0,2,1:T(8,128)(2,1)} %constant_dynamic-slice_fusion.18) | copy-start | bytes 196612
  96.2 17.5 %copy-start.22 = (s32[1,64,4]{1,2,0:T(4,128)S(1)}, s32[1,64,4]{1,2,0:T(4,128)}, u32[]{:S(2)}) copy-start(s32[1,64,4]{1,2,0:T(4,128)} %param.39) | copy-start | bytes 3076
  96.2 24.1 %copy-start.14 = (bf16[128,256]{1,0:T(8,128)(2,1)S(1)}, bf16[128,256]{1,0:T(8,128)(2,1)}, u32[]{:S(2)}) copy-start(bf16[128,256]{1,0:T(8,128)(2,1)} %param.33) | copy-start | bytes 196612
  96.3 24.3 %copy-start.7 = (bf16[128,256]{1,0:T(8,128)(2,1)S(1)}, bf16[128,256]{1,0:T(8,128)(2,1)}, u32[]{:S(2)}) copy-start(bf16[128,256]{1,0:T(8,128)(2,1)} %param.36) | copy-start | bytes 196612
  96.3 621.5 %all-to-all-start = ((bf16[32,128,256]{2,1,0:T(8,128)(2,1)}), bf16[32,128,256]{2,1,0:T(8,128)(2,1)}, u32[]{:S(2)}, u32[]{:S(2)}) async-start(bf16[32,128,256]{2,1,0:T(8,128)(2,1)} %stack.5), calls=%async_computation | async-start | bytes 4194304 | tf_op jit(solution)/shard_map/all_to_all | solution.py:200
  113.2 611.6 %all-reduce.5.cloned.1.call-start = ((), (), s32[]{:S(2)}) async-start(), calls=%async_computation.8 | async-start | bytes 1048576 | tf_op jit(solution)/shard_map/psum | solution.py:263
  115.7 5.6 copy-start.28
  116.5 4.9 copy-start.23
  117.0 3.4 copy-start.31
  117.0 3.4 copy-start.20
  121.3 67.3 %copy-start.21 = (f32[1,4096]{1,0:T(1,128)S(1)}, f32[1,4096]{1,0:T(1,128)}, u32[]{:S(2)}) copy-start(f32[1,4096]{1,0:T(1,128)} %param.38) | copy-start | bytes 49156
  188.7 2.6 copy-start.4
  191.3 1.6 copy-start.3
  628.7 0.6 copy-start.12
  628.8 0.7 copy-start.17
  628.8 0.7 copy-start.32
  629.5 26.6 %copy-start.13 = (pred[64,64]{1,0:T(8,128)(4,1)S(1)}, pred[64,64]{1,0:T(8,128)(4,1)}, u32[]{:S(2)}) copy-start(pred[64,64]{1,0:T(8,128)(4,1)} %iota_compare_fusion.16) | copy-start | bytes 12292
  656.1 54.7 %copy-start.8 = (bf16[128,128]{1,0:T(8,128)(2,1)S(1)}, bf16[128,128]{1,0:T(8,128)(2,1)}, u32[]{:S(2)}) copy-start(bf16[128,128]{1,0:T(8,128)(2,1)} %param.41) | copy-start | bytes 98308
  656.1 55.6 %copy-start.9 = (bf16[128,128]{1,0:T(8,128)(2,1)S(1)}, bf16[128,128]{1,0:T(8,128)(2,1)}, u32[]{:S(2)}) copy-start(bf16[128,128]{1,0:T(8,128)(2,1)} %param.40) | copy-start | bytes 98308
  656.1 22.7 %copy-start.33 = (f32[2,2,1,1]{1,3,2,0:T(1,128)}, f32[2,2,1,1]{1,3,2,0:T(1,128)S(1)}, u32[]{:S(2)}) copy-start(f32[2,2,1,1]{1,3,2,0:T(1,128)S(1)} %get-tuple-element.4409) | copy-start | bytes 52 | tf_op jit(solution)/shard_map/transpose(jvp())/while
  679.3 4.0 copy-start.34
  683.3 22.7 %copy-start.33 = (f32[2,2,1,1]{1,3,2,0:T(1,128)}, f32[2,2,1,1]{1,3,2,0:T(1,128)S(1)}, u32[]{:S(2)}) copy-start(f32[2,2,1,1]{1,3,2,0:T(1,128)S(1)} %get-tuple-element.4409) | copy-start | bytes 52 | tf_op jit(solution)/shard_map/transpose(jvp())/while
  706.5 4.0 copy-start.34
  710.5 10.7 %copy-start.6 = (bf16[8,64,256]{2,1,0:T(8,128)(2,1)S(1)}, bf16[8,64,256]{2,1,0:T(8,128)(2,1)}, u32[]{:S(2)}) copy-start(bf16[8,64,256]{2,1,0:T(8,128)(2,1)} %gather_fusion.1) | copy-start | bytes 786436
  710.5 11.9 %copy-start.10 = (f32[2,2,64,128]{3,2,1,0:T(8,128)S(1)}, f32[2,2,64,128]{3,2,1,0:T(8,128)}, u32[]{:S(2)}) copy-start(f32[2,2,64,128]{3,2,1,0:T(8,128)} %get-tuple-element.2079) | copy-start | bytes 393220
  710.5 12.6 %copy-start.25 = (f32[128]{0:T(128)S(1)}, f32[128]{0:T(128)}, u32[]{:S(2)}) copy-start(f32[128]{0:T(128)} %copy-done.24) | copy-start | bytes 1540
  710.5 13.4 %copy-start.15 = (f32[2,64,64]{1,2,0:T(8,128)S(1)}, f32[2,64,64]{1,2,0:T(8,128)}, u32[]{:S(2)}) copy-start(f32[2,64,64]{1,2,0:T(8,128)} %fusion.283) | copy-start | bytes 98308
Sparse Core Ops, SparseCore 0:
  10.1 78.4 all-gather.12
  90.8 97.8 all-gather.14
  191.3 72.5 all-gather.16
  266.5 71.1 all-gather.20
  340.2 70.1 all-gather.18
  412.4 70.7 all-gather.24
  485.3 69.7 all-gather.22
  558.9 111.2 all-reduce.4
